TPU v7x, 128 devices: a whole 4x4x4 slice. The times are simulated.
128 devices in a mesh: grp: 4 (over y_lo, core), band: 32 (over y_hi, x, z).
Axes of the slice: x: 4, y: 4 (y_hi: 2, y_lo: 2; y = y_hi * 2 + y_lo), z: 4, core: 2. Of those that a mesh axis runs over, the one named last changes fastest.
Arguments:
- prior_samples: bfloat16 [32, 69, 64, 1024], P('grp', None, 'band'), may hold values from -6 to 6
- conv1_weight: bfloat16 [3, 3, 256, 69], replicated, may hold values from -0.25 to 0.25
- conv1_bias: float32 [256], replicated, may hold values from -3 to 3
- conv2_weight: bfloat16 [3, 3, 69, 256], replicated, may hold values from -0.125 to 0.125
- conv2_bias: float32 [69], replicated, may hold values from -3 to 3
- obs_index: int32 [256, 256], P(('grp', 'band')), may hold values from 0 to 17663
- obs_values: float32 [256, 256], P(('grp', 'band')), may hold values from -6 to 6
- obs_prec: float32 [256, 256], P(('grp', 'band')), may hold values from 0.25 to 4
- neighbours: int32 [256, 8], P(('grp', 'band')), may hold values from 0 to 255
- loc_weight: float32 [256, 8], P(('grp', 'band')), may hold values from 0.2 to 1
Outputs:
- analysis: float32 [32, 69, 64, 1024], P(None, None, 'band', 'grp')
Inputs may be any that keep to these rules, and one draw needn't show every extreme that they name: `neighbours`: neighbour patch numbers; a number may repeat or name the patch itself. `obs_index`: observed entry as channel * 256 + column within the patch.
All inputs are finite; a program needn't handle non-finite values.
Results may differ from a plain program's by a relative error of at most 0.0021.
Values may be sent and summed in bfloat16 or wider, within the bound.
No kernel may reach another device: no remote copies, remote signals or barrier semaphores. Data moves between devices by JAX's collectives and lax.ppermute only.
A program may use at most 128 MiB of HBM per device.

v0:
```python
import jax
import jax.numpy as jnp
from jax import lax
from jax.sharding import PartitionSpec as P

NS_ITERS = 6


def padded_2(cells, sides, width):
    for axis, dim in sides:
        count = lax.axis_size(axis)
        ends = count - 1
        head = lax.slice_in_dim(cells, 0, width, axis=dim)
        tail = lax.slice_in_dim(cells, cells.shape[dim] - width, cells.shape[dim], axis=dim)
        cells = jnp.concatenate(
            [
                lax.ppermute(tail, axis, [(i, (i + 1) % count) for i in range(ends)]),
                cells,
                lax.ppermute(head, axis, [((i + 1) % count, i) for i in range(ends)]),
            ],
            axis=dim,
        )
    return cells


def from_behind(block, axis, distance):
    devices = range(lax.axis_size(axis))
    route = [(i - distance, i) for i in devices if i - distance in devices]
    return lax.ppermute(block, axis, route)


def convolve(padded, kernel, height):
    summed = jnp.zeros((kernel.shape[2], height, padded.shape[2]), jnp.float32)
    for row_shift in range(3):
        window = padded[:, row_shift : row_shift + height, :]
        for col_shift in range(3):
            shifted = jnp.roll(window, 1 - col_shift, axis=2)
            summed = summed + jnp.einsum(
                "oc,crl->orl",
                kernel[row_shift, col_shift],
                shifted,
                preferred_element_type=jnp.float32,
            )
    return summed


def grams_of(perturb, obs_prec, innovation):
    highest = lax.Precision.HIGHEST
    gram_local = jnp.einsum("pmo,po,pno->pmn", perturb, obs_prec, perturb, precision=highest)
    pull_vec = jnp.einsum("pmo,po->pm", perturb, obs_prec * innovation, precision=highest)
    return (gram_local, pull_vec)


def on_device(
    prior_samples,
    conv1_weight,
    conv1_bias,
    conv2_weight,
    conv2_bias,
    obs_index,
    obs_values,
    obs_prec,
    neighbours,
    loc_weight,
):
    highest = lax.Precision.HIGHEST
    height = prior_samples.shape[2]
    padded = padded_2(prior_samples, (("band", 2),), 1)

    def first_layer(member):
        return jax.nn.silu(
            convolve(member, conv1_weight, height) + conv1_bias[:, None, None]
        ).astype(jnp.bfloat16)

    hidden_fields = lax.map(first_layer, padded)
    northern_halo = from_behind(hidden_fields[:, :, height - 1 :, :], "band", 1)
    southern_halo = from_behind(hidden_fields[:, :, :1, :], "band", -1)

    def output_layer(inputs):
        member, own_rows, above_row, below_row = inputs
        extended = jnp.concatenate([above_row, own_rows, below_row], axis=1)
        summed = (
            member.astype(jnp.float32)
            + convolve(extended, conv2_weight, height)
            + conv2_bias[:, None, None]
        )
        return summed.astype(jnp.bfloat16)

    predicted_samples = lax.map(
        output_layer, (prior_samples, hidden_fields, northern_halo, southern_halo)
    )
    patch_block_slice = lax.all_to_all(
        predicted_samples, "grp", split_axis=3, concat_axis=0, tiled=True
    )
    ensemble = patch_block_slice.shape[0]
    channels = patch_block_slice.shape[1]
    patch_width = patch_block_slice.shape[3]
    realization_grid = jnp.transpose(patch_block_slice, (2, 0, 1, 3)).reshape(
        height, ensemble, channels * patch_width
    )
    count_obs = obs_index.shape[1]
    chosen = jnp.broadcast_to(obs_index[:, None, :], (height, ensemble, count_obs))
    predicted = jnp.take_along_axis(realization_grid, chosen, axis=2).astype(jnp.float32)
    predicted_mean = jnp.mean(predicted, axis=1)
    perturb = predicted - predicted_mean[:, None, :]
    innovation = obs_values - predicted_mean
    gram_local, pull_vec = grams_of(perturb, obs_prec, innovation)
    total_patches = height * lax.axis_size("grp") * lax.axis_size("band")
    patch_ids = jnp.arange(total_patches, dtype=jnp.int32)
    matches = (neighbours[:, :, None] == patch_ids[None, None, :]).astype(jnp.float32)
    spread_weights = jnp.sum(loc_weight[:, :, None] * matches, axis=1)
    piece_gram, piece_pull = grams_of(
        lax.all_gather(perturb, ("grp", "band"), axis=0, tiled=True),
        lax.all_gather(obs_prec, ("grp", "band"), axis=0, tiled=True),
        lax.all_gather(innovation, ("grp", "band"), axis=0, tiled=True),
    )
    gram_sum = jnp.einsum("pj,jab->pab", spread_weights, piece_gram, precision=highest)
    pull_sum = jnp.einsum("pj,ja->pa", spread_weights, piece_pull, precision=highest)
    identity = jnp.broadcast_to(jnp.eye(ensemble, dtype=jnp.float32), (height, ensemble, ensemble))
    matrix = (ensemble - 1.0) * identity + gram_local + gram_sum
    pulled = pull_vec + pull_sum
    norm_scale = jnp.sqrt(jnp.sum(matrix * matrix, axis=(1, 2)))
    sqrt_iter = matrix / norm_scale[:, None, None]
    inverse_root = identity
    for sweep in range(NS_ITERS):
        half_step = 1.5 * identity - 0.5 * jnp.einsum(
            "pab,pbc->pac", inverse_root, sqrt_iter, precision=highest
        )
        sqrt_iter = jnp.einsum("pab,pbc->pac", sqrt_iter, half_step, precision=highest)
        inverse_root = jnp.einsum("pab,pbc->pac", half_step, inverse_root, precision=highest)
    once_applied = jnp.einsum("pab,pb->pa", inverse_root, pulled, precision=highest)
    mean_weight = (
        jnp.einsum("pab,pb->pa", inverse_root, once_applied, precision=highest)
        / norm_scale[:, None]
    )
    transform = (jnp.sqrt(ensemble - 1.0) / jnp.sqrt(norm_scale))[
        :, None, None
    ] * inverse_root + mean_weight[:, :, None]
    field = realization_grid.astype(jnp.float32)
    centre = jnp.mean(field, axis=1)
    spread = field - centre[:, None, :]
    analysed = centre[:, None, :] + jnp.einsum("pkm,pkc->pmc", transform, spread, precision=highest)
    return analysed.reshape(height, ensemble, channels, patch_width).transpose(1, 2, 0, 3)


def solution(mesh):
    placed = (
        P("grp", None, "band", None),
        P(),
        P(),
        P(),
        P(),
        P(("grp", "band"), None),
        P(("grp", "band"), None),
        P(("grp", "band"), None),
        P(("grp", "band"), None),
        P(("grp", "band"), None),
    )
    return jax.shard_map(
        on_device,
        mesh=mesh,
        in_specs=placed,
        out_specs=P(None, None, "band", "grp"),
        check_vma=False,
    )
```

profile of v0, /device:TPU:48, one launch (start us, length us, event | category | flops | bytes accessed | tf_op | source)
XLA Modules:
  0.0 1311.0 jit_solution(5187582412730233797)
XLA Ops:
  6.5 5.9 fusion.156
  12.9 4.0 collective-permute-start
  16.9 1.4 copy.95
  18.3 2.0 collective-permute-start.1
  21.0 20.6 %collective-permute-done = bf16[8,69,1,1024]{3,0,2,1:T(8,128)(2,1)} collective-permute-done((bf16[8,69,1,1024]{3,0,2,1:T(8,128)(2,1)S(1)}, bf16[8,69,1,1024]{3,0,2,1:T(8,128)(2,1)}, u32[]{:S(2)}, u32[]{:S(2)}) %collective-permute-start) | collective-permute-done | bytes 1130528 | tf_op jit(solution)/shard_map/ppermute | solution.py:17
  41.7 1.9 copy.66
  43.6 3.3 collective-permute-done.1
  46.8 1.9 copy.68
  48.7 2.5 pad_maximum_fusion.6
  51.3 73.3 %while.20 = (s32[]{:T(128)}, bf16[8,256,2,1024]{3,1,2,0:T(8,128)(2,1)}, bf16[8,69,4,1024]{3,1,2,0:T(8,128)(2,1)}, bf16[3,3,256,69]{2,3,1,0:T(8,128)(2,1)S(1)}, f32[256]{0:T(256)S(1)}, /*index=5*/s32[]{:T(128)}) while((s32[]{:T(128)}, bf16[8,256,2,1024]{3,1,2,0:T(8,128)(2,1)}, bf16[8,69,4,1024]{3,1,2,0:T(8,128)(2,1)}, ...), condition=%wide.region_1.2_spmd, body=%wide.region_0.1_spmd.sunk | while | flops 661897216 | bytes 47412808 | solution.py:75
  124.5 6.1 fusion.155
  130.6 3.5 collective-permute-start.2
  134.1 4.2 collective-permute-start.3
  138.4 87.3 %collective-permute-done.2 = bf16[8,256,1,1024]{3,1,2,0:T(8,128)(2,1)} collective-permute-done((bf16[8,256,1,1024]{3,1,2,0:T(8,128)(2,1)}, bf16[8,256,1,1024]{3,1,2,0:T(8,128)(2,1)}, u32[]{:S(2)}, u32[]{:S(2)}) %collective-permute-start.2) | collective-permute-done | bytes 4194336 | tf_op jit(solution)/shard_map/ppermute | solution.py:29
  225.7 2.4 collective-permute-done.3
  228.0 70.6 %while.21 = (s32[]{:T(128)}, bf16[8,69,2,1024]{3,1,2,0:T(8,128)(2,1)S(1)}, bf16[8,69,2,1024]{3,1,2,0:T(8,128)(2,1)}, bf16[8,256,1,1024]{3,1,2,0:T(8,128)(2,1)}, ...) while((s32[]{:T(128)}, ...), condition=%wide.region_3.4_spmd, body=%wide.region_2.3_spmd.sunk | while | flops 675929088 | bytes 41343592 | solution.py:89
  298.6 7.7 copy.73
  306.3 5.0 all-to-all-start
  311.4 48.1 %all-to-all-done = bf16[8,69,2,1024]{1,2,0,3:T(2,128)(2,1)} async-done(((bf16[8,69,2,1024]{1,2,0,3:T(2,128)(2,1)}), bf16[8,69,2,1024]{1,2,0,3:T(2,128)(2,1)}, u32[]{:S(2)}, u32[]{:S(2)}) %all-to-all-start) | async-done | bytes 2261024 | tf_op jit(solution)/shard_map/all_to_all | solution.py:92
  359.5 10.5 copy.90
  370.0 2.7 copy.91
  372.7 3.1 reshape.45
  375.9 159.3 %gather_fusion = bf16[16384]{0:T(1024)(128)(2,1)S(1)} fusion(bf16[2,32,17664]{2,1,0:T(8,128)(2,1)S(1)} %reshape.45, s32[16384]{0:T(1024)S(1)} %bitcast.273), kind=kCustom, calls=%fused_computation | custom fusion | bytes 262144 | tf_op jit(solution)/shard_map/jit(take_along_axis)/gather | solution.py:103
  535.9 356.6 %all-gather = f32[128,2,256]{2,1,0:T(2,128)S(1)} all-gather(f32[1,2,256]{2,1,0:T(2,128)S(1)} %bitcast.281), channel_id=1, replica_groups=mesh['grp'=4,'band'=32] {'grp','band'}, dimensions={0}, use_global_device_ids=true | all-gather | bytes 264192 | tf_op jit(solution)/shard_map/all_gather | solution.py:114
  892.8 356.1 %all-gather.1 = f32[128,2,256]{2,1,0:T(2,128)S(1)} all-gather(f32[1,2,256]{2,1,0:T(2,128)S(1)} %get-tuple-element.172), channel_id=1, replica_groups=mesh['grp'=4,'band'=32] {'grp','band'}, dimensions={0}, use_global_device_ids=true | all-gather | bytes 264192 | tf_op jit(solution)/shard_map/all_gather | solution.py:115
  1249.3 2.9 convert_reduce_fusion
  1252.3 14.7 %fusion.116 = f32[256,32,32]{2,1,0:T(8,128)S(1)} fusion(f32[256,32,256]{2,1,0:T(8,128)} %all-gather.4.cloned.1.call-done, f32[256,256]{1,0:T(8,128)S(1)} %reshape.55), kind=kOutput, calls=%fused_computation.146 | convolution fusion | flops 807403520 | bytes 9699328 | tf_op jit(solution)/shard_map/pmo,po,pno->pmn/dot_general | solution.py:49
  1267.0 4.3 fusion.120
  1274.7 9.9 fusion.131
  1285.2 5.6 convolution_add_fusion.7
  1290.8 5.1 reshape.46
  1296.0 7.9 copy.80
  (287 shorter events, 149.5 us)
Async XLA Ops:
  12.9 7.4 copy-start
  12.9 28.8 %collective-permute-start = (bf16[8,69,1,1024]{3,0,2,1:T(8,128)(2,1)S(1)}, bf16[8,69,1,1024]{3,0,2,1:T(8,128)(2,1)}, u32[]{:S(2)}, u32[]{:S(2)}) collective-permute-start(bf16[8,69,1,1024]{3,0,2,1:T(8,128)(2,1)S(1)} %copy.94), channel_id=1, source_target_pairs={{0,1},{1,2},{2,3},{3,4},{4,5},{5,6},{6,7},{7,8},{8,9},{9,10},{10,1... | collective-permute-start | bytes 3391496 | tf_op jit(solution)/shard_map/ppermute | solution.py:17
  18.3 28.6 %collective-permute-start.1 = (bf16[8,69,1,1024]{3,0,2,1:T(8,128)(2,1)}, bf16[8,69,1,1024]{3,0,2,1:T(8,128)(2,1)}, u32[]{:S(2)}, u32[]{:S(2)}) collective-permute-start(bf16[8,69,1,1024]{3,0,2,1:T(8,128)(2,1)} %copy.95), channel_id=1, source_target_pairs={{1,0},{2,1},{3,2},{4,3},{5,4},{6,5},{7,6},{8,7},{9,8},{10,9},{11,1... | collective-permute-start | bytes 3391496 | tf_op jit(solution)/shard_map/ppermute | solution.py:19
  21.0 27.7 %copy-start.2 = (bf16[8,69,2,1024]{3,1,2,0:T(8,128)(2,1)}, bf16[8,69,2,1024]{3,1,2,0:T(8,128)(2,1)S(1)}, u32[]{:S(2)}) copy-start(bf16[8,69,2,1024]{3,1,2,0:T(8,128)(2,1)S(1)} %copy.71) | copy-start | bytes 6782980
  48.7 2.6 copy-start.3
  48.7 2.5 copy-start.6
  124.5 103.5 %copy-start.4 = (bf16[3,3,69,256]{3,2,1,0:T(8,128)(2,1)S(1)}, bf16[3,3,69,256]{3,2,1,0:T(8,128)(2,1)}, u32[]{:S(2)}) copy-start(bf16[3,3,69,256]{3,2,1,0:T(8,128)(2,1)} %param.17) | copy-start | bytes 953860
  124.5 103.5 %copy-start.11 = (f32[69]{0:T(128)S(1)}, f32[69]{0:T(128)}, u32[]{:S(2)}) copy-start(f32[69]{0:T(128)} %param.18) | copy-start | bytes 832
  130.6 95.0 %collective-permute-start.2 = (bf16[8,256,1,1024]{3,1,2,0:T(8,128)(2,1)}, bf16[8,256,1,1024]{3,1,2,0:T(8,128)(2,1)}, u32[]{:S(2)}, u32[]{:S(2)}) collective-permute-start(bf16[8,256,1,1024]{3,1,2,0:T(8,128)(2,1)} %get-tuple-element.169), channel_id=1, source_target_pairs={{0,1},{1,2},{2,3},{3,4},{4,5},{5,6},{6,7},{7,8},{8,9},{9,10},{10,1... | collective-permute-start | bytes 12582920 | tf_op jit(solution)/shard_map/ppermute | solution.py:29
  134.1 93.9 %collective-permute-start.3 = (bf16[8,256,1,1024]{3,1,2,0:T(8,128)(2,1)}, bf16[8,256,1,1024]{3,1,2,0:T(8,128)(2,1)}, u32[]{:S(2)}, u32[]{:S(2)}) collective-permute-start(bf16[8,256,1,1024]{3,1,2,0:T(8,128)(2,1)} %get-tuple-element.168), channel_id=1, source_target_pairs={{1,0},{2,1},{3,2},{4,3},{5,4},{6,5},{7,6},{8,7},{9,8},{10,9},{11,1... | collective-permute-start | bytes 12582920 | tf_op jit(solution)/shard_map/ppermute | solution.py:29
  306.3 5.0 copy-start.5
  306.3 53.2 %all-to-all-start = ((bf16[8,69,2,1024]{1,2,0,3:T(2,128)(2,1)}), bf16[8,69,2,1024]{1,2,0,3:T(2,128)(2,1)}, u32[]{:S(2)}, u32[]{:S(2)}) async-start(bf16[8,69,2,1024]{1,2,0,3:T(2,128)(2,1)} %copy.73), calls=%async_computation | async-start | bytes 8388608 | tf_op jit(solution)/shard_map/all_to_all | solution.py:92
  311.3 941.0 %all-gather.4.cloned.1.call-start = ((), (), s32[]{:S(2)}) async-start(), calls=%async_computation.1 | async-start | bytes 8454144 | tf_op jit(solution)/shard_map/all_gather | solution.py:113
  370.0 2.7 copy-start.1
  375.8 159.4 %copy-start.7 = (f32[2,256]{1,0:T(2,128)S(1)}, f32[2,256]{1,0:T(2,128)}, u32[]{:S(2)}) copy-start(f32[2,256]{1,0:T(2,128)} %param.21) | copy-start | bytes 6148
  375.8 159.4 %copy-start.8 = (f32[2,256]{1,0:T(2,128)S(1)}, f32[2,256]{1,0:T(2,128)}, u32[]{:S(2)}) copy-start(f32[2,256]{1,0:T(2,128)} %param.20) | copy-start | bytes 6148
  375.8 516.9 %copy-start.9 = (f32[2,8]{1,0:T(2,128)S(1)}, f32[2,8]{1,0:T(2,128)}, u32[]{:S(2)}) copy-start(f32[2,8]{1,0:T(2,128)} %param.23) | copy-start | bytes 196
  375.8 516.9 %copy-start.10 = (s32[2,8]{1,0:T(2,128)S(1)}, s32[2,8]{1,0:T(2,128)}, u32[]{:S(2)}) copy-start(s32[2,8]{1,0:T(2,128)} %param.22) | copy-start | bytes 196
Sparse Core Ops, SparseCore 0:
  536.0 320.7 all-gather.3
where the time goes:
time: 1320 us; the launch traced here: 1310 us
  blocking collectives  713 us (54%)
  local copies, waits for them, and re-layouts  261 us (20%)
  waiting for transfers between devices  162 us (12%)
  matrix products  123 us (9%)
  starting transfers between devices  18.7 us (1%)
  other arithmetic  18.6 us (1%)
  between operations  14.1 us (1%)
    all_gather x1, blocking collectives, on_device(): lax.all_gather(obs_prec, ('grp', 'band'), axis=0, tiled=True)  357 us
    all_gather x1, blocking collectives, on_device(): lax.all_gather(innovation, ('grp', 'band'), axis=0, tiled=True)  356 us
    gather x2, local copies, waits for them, and re-layouts, on_device(): jnp.take_along_axis(realization_grid, chosen, axis=2).astype(jnp.float32)  159 us
    ppermute x2, waiting for transfers between devices, from_behind(): return lax.ppermute(block, axis, route)  89.7 us
    dot_general x144, matrix products, convolve(): jnp.einsum('oc,crl->orl', kernel[row_shift, col_shift], shifted, preferre...  84.6 us
    all_to_all x1, waiting for transfers between devices, on_device(): lax.all_to_all(predicted_samples, 'grp', split_axis=3, concat_axis=0, til...  48.1 us
  transfers between devices with their start and end apart: 6, of which 5 were waited for; matrix products, arithmetic and copies ran while one was open for 1% of the time, Pallas kernels for 0%

commit v1 on v0

--- a/solution.py
+++ b/solution.py
@@ -63,6 +63,13 @@
     neighbours,
     loc_weight,
 ):
+
+    def fill_the_frame(slab_in):
+        k_now = jnp.stack([slab_in for _ in range(jax.lax.psum(1, axis_name=("grp", "band")))])
+        inter = jax.lax.all_to_all(k_now, axis_name=("grp", "band"), split_axis=0, concat_axis=0)
+        next_value = jnp.concatenate(inter, 0)
+        return next_value
+
     highest = lax.Precision.HIGHEST
     height = prior_samples.shape[2]
     padded = padded_2(prior_samples, (("band", 2),), 1)
@@ -111,7 +118,7 @@
     spread_weights = jnp.sum(loc_weight[:, :, None] * matches, axis=1)
     piece_gram, piece_pull = grams_of(
         lax.all_gather(perturb, ("grp", "band"), axis=0, tiled=True),
-        lax.all_gather(obs_prec, ("grp", "band"), axis=0, tiled=True),
+        fill_the_frame(obs_prec),
         lax.all_gather(innovation, ("grp", "band"), axis=0, tiled=True),
     )
     gram_sum = jnp.einsum("pj,jab->pab", spread_weights, piece_gram, precision=highest)

time: 1320 us -> 996 us (0.75)
  blocking collectives: 713 us -> 350 us
  starting transfers between devices: 18.7 us -> 35.1 us
    all_gather x1 -> x0, blocking collectives: 357 us -> none  [on_device(): lax.all_gather(obs_prec, ('grp', 'band'), axis=0, tiled=True)]
    all_to_all x0 -> x1, starting transfers between devices: none -> 16.3 us  [fill_the_frame(): jax.lax.all_to_all(k_now, axis_name=('grp', 'band'), split_axis=0, concat...]
  transfers between devices with their start and end apart: 6 -> 7, of which waited for: 5 -> 6; matrix products, arithmetic and copies ran while one was open for 1% -> 1% of each run, Pallas kernels for 0% -> 0%
where the time goes in v1:
time: 996 us; the launch traced here: 984 us
  blocking collectives  350 us (35%)
  local copies, waits for them, and re-layouts  267 us (27%)
  waiting for transfers between devices  169 us (17%)
  matrix products  129 us (13%)
  starting transfers between devices  35.1 us (4%)
  other arithmetic  18.8 us (2%)
  between operations  14.1 us (1%)
    all_gather x1, blocking collectives, on_device(): lax.all_gather(innovation, ('grp', 'band'), axis=0, tiled=True)  350 us
    gather x2, local copies, waits for them, and re-layouts, on_device(): jnp.take_along_axis(realization_grid, chosen, axis=2).astype(jnp.float32)  159 us
    dot_general x144, matrix products, convolve(): jnp.einsum('oc,crl->orl', kernel[row_shift, col_shift], shifted, preferre...  90.8 us
    ppermute x2, waiting for transfers between devices, from_behind(): return lax.ppermute(block, axis, route)  89.7 us
    all_to_all x1, waiting for transfers between devices, on_device(): lax.all_to_all(predicted_samples, 'grp', split_axis=3, concat_axis=0, til...  48.1 us
    squeeze x16, local copies, waits for them, and re-layouts, on_device(): lax.map(output_layer, (prior_samples, hidden_fields, northern_halo, south...  20.5 us
  transfers between devices with their start and end apart: 7, of which 6 were waited for; matrix products, arithmetic and copies ran while one was open for 1% of the time, Pallas kernels for 0%

profile of v1, /device:TPU:48, one launch (start us, length us, event | category | flops | bytes accessed | tf_op | source)
XLA Modules:
  0.0 983.9 jit_solution(92971103019147899)
XLA Ops:
  6.5 6.0 fusion.156
  13.0 4.0 collective-permute-start
  20.4 2.2 copy.71
  22.6 19.2 %collective-permute-done = bf16[8,69,1,1024]{3,0,2,1:T(8,128)(2,1)} collective-permute-done((bf16[8,69,1,1024]{3,0,2,1:T(8,128)(2,1)S(1)}, bf16[8,69,1,1024]{3,0,2,1:T(8,128)(2,1)}, u32[]{:S(2)}, u32[]{:S(2)}) %collective-permute-start) | collective-permute-done | bytes 1130528 | tf_op jit(solution)/shard_map/ppermute | solution.py:17
  43.7 3.3 collective-permute-done.1
  48.9 2.5 pad_maximum_fusion.6
  51.4 73.4 %while.20 = (s32[]{:T(128)}, bf16[8,256,2,1024]{3,1,2,0:T(8,128)(2,1)}, bf16[8,69,4,1024]{3,1,2,0:T(8,128)(2,1)}, bf16[3,3,256,69]{2,3,1,0:T(8,128)(2,1)S(1)}, f32[256]{0:T(256)S(1)}, /*index=5*/s32[]{:T(128)}) while((s32[]{:T(128)}, bf16[8,256,2,1024]{3,1,2,0:T(8,128)(2,1)}, bf16[8,69,4,1024]{3,1,2,0:T(8,128)(2,1)}, ...), condition=%wide.region_1.2_spmd, body=%wide.region_0.1_spmd.sunk | while | flops 661897216 | bytes 47412808 | solution.py:82
  124.8 6.0 fusion.155
  130.8 3.5 collective-permute-start.2
  134.3 4.2 collective-permute-start.3
  138.6 87.3 %collective-permute-done.2 = bf16[8,256,1,1024]{3,1,2,0:T(8,128)(2,1)} collective-permute-done((bf16[8,256,1,1024]{3,1,2,0:T(8,128)(2,1)}, bf16[8,256,1,1024]{3,1,2,0:T(8,128)(2,1)}, u32[]{:S(2)}, u32[]{:S(2)}) %collective-permute-start.2) | collective-permute-done | bytes 4194336 | tf_op jit(solution)/shard_map/ppermute | solution.py:29
  225.9 2.4 collective-permute-done.3
  228.2 76.5 %while.21 = (s32[]{:T(128)}, bf16[8,69,2,1024]{3,1,2,0:T(8,128)(2,1)}, bf16[8,69,2,1024]{3,1,2,0:T(8,128)(2,1)}, bf16[8,256,1,1024]{3,1,2,0:T(8,128)(2,1)}, bf16...) while((s32[]{:T(128)}, ...), condition=%wide.region_3.4_spmd, body=%wide.region_2.3_spmd.sunk | while | flops 675929088 | bytes 41356388 | solution.py:96
  283.6 2.0 fusion.310
  302.8 2.0 fusion.310
  304.8 10.9 %copy.73 = bf16[8,69,2,1024]{1,2,0,3:T(2,128)(2,1)} copy(bf16[8,69,2,1024]{3,1,2,0:T(8,128)(2,1)} %get-tuple-element.75) | data formatting | bytes 4521984 | tf_op jit(solution)/shard_map/while | solution.py:96
  315.7 5.0 all-to-all-start
  320.8 48.1 %all-to-all-done = bf16[8,69,2,1024]{1,2,0,3:T(2,128)(2,1)} async-done(((bf16[8,69,2,1024]{1,2,0,3:T(2,128)(2,1)}), bf16[8,69,2,1024]{1,2,0,3:T(2,128)(2,1)}, u32[]{:S(2)}, u32[]{:S(2)}) %all-to-all-start) | async-done | bytes 2261024 | tf_op jit(solution)/shard_map/all_to_all | solution.py:99
  368.9 10.5 %copy.90 = bf16[8,69,2,4,256]{4,3,0,2,1:T(4,128)(2,1)S(1)} copy(bf16[8,69,2,4,256]{1,2,0,4,3:T(2,128)(2,1)} %bitcast.45) | data formatting | bytes 4521984 | tf_op jit(solution)/shard_map/all_to_all | solution.py:99
  379.4 2.7 copy.91
  382.1 3.1 reshape.50
  385.3 159.3 %gather_fusion = bf16[16384]{0:T(1024)(128)(2,1)S(1)} fusion(bf16[2,32,17664]{2,1,0:T(8,128)(2,1)S(1)} %reshape.50, s32[16384]{0:T(1024)S(1)} %bitcast.272), kind=kCustom, calls=%fused_computation | custom fusion | bytes 262144 | tf_op jit(solution)/shard_map/jit(take_along_axis)/gather | solution.py:110
  546.0 16.3 %all-to-all-start.1 = ((f32[128,2,256]{2,1,0:T(2,128)}), f32[128,2,256]{2,1,0:T(2,128)S(1)}, u32[]{:S(2)}, u32[]{:S(2)}) async-start(f32[128,2,256]{2,1,0:T(2,128)} %stack.2), calls=%async_computation.1 | async-start | bytes 524288 | tf_op jit(solution)/shard_map/all_to_all | solution.py:69
  562.5 9.0 all-to-all-done.1
  571.7 350.1 %all-gather = f32[128,2,256]{2,1,0:T(2,128)S(1)} all-gather(f32[1,2,256]{2,1,0:T(2,128)S(1)} %get-tuple-element.172), channel_id=1, replica_groups=mesh['grp'=4,'band'=32] {'grp','band'}, dimensions={0}, use_global_device_ids=true | all-gather | bytes 264192 | tf_op jit(solution)/shard_map/all_gather | solution.py:122
  922.2 2.9 convert_reduce_fusion
  925.2 14.6 %fusion.116 = f32[256,32,32]{2,1,0:T(8,128)S(1)} fusion(f32[256,32,256]{2,1,0:T(8,128)} %all-gather.3.cloned.1.call-done, f32[256,256]{1,0:T(8,128)S(1)} %reshape.51), kind=kOutput, calls=%fused_computation.146 | convolution fusion | flops 807403520 | bytes 9699328 | tf_op jit(solution)/shard_map/pmo,po,pno->pmn/dot_general | solution.py:49
  939.8 4.3 fusion.120
  947.5 9.9 %fusion.131 = f32[256,1,32]{2,1,0:T(1,128)S(1)} fusion(f32[256,32,256]{2,1,0:T(8,128)} %all-gather.3.cloned.1.call-done, f32[256,256,1]{1,0,2:T(8,128)S(1)} %multiply_bitcast_fusion), kind=kOutput, calls=%fused_computation.172 | convolution fusion | flops 25165824 | bytes 8683520 | tf_op jit(solution)/shard_map/pmo,po->pm/dot_general | solution.py:50
  958.1 5.6 convolution_add_fusion.7
  963.7 5.2 reshape.52
  968.9 7.9 copy.80
  (289 shorter events, 158.9 us)
Async XLA Ops:
  13.0 7.4 copy-start
  13.0 28.8 %collective-permute-start = (bf16[8,69,1,1024]{3,0,2,1:T(8,128)(2,1)S(1)}, bf16[8,69,1,1024]{3,0,2,1:T(8,128)(2,1)}, u32[]{:S(2)}, u32[]{:S(2)}) collective-permute-start(bf16[8,69,1,1024]{3,0,2,1:T(8,128)(2,1)S(1)} %copy.94), channel_id=1, source_target_pairs={{0,1},{1,2},{2,3},{3,4},{4,5},{5,6},{6,7},{7,8},{8,9},{9,10},{10,1... | collective-permute-start | bytes 3391496 | tf_op jit(solution)/shard_map/ppermute | solution.py:17
  18.4 28.6 %collective-permute-start.1 = (bf16[8,69,1,1024]{3,0,2,1:T(8,128)(2,1)}, bf16[8,69,1,1024]{3,0,2,1:T(8,128)(2,1)}, u32[]{:S(2)}, u32[]{:S(2)}) collective-permute-start(bf16[8,69,1,1024]{3,0,2,1:T(8,128)(2,1)} %copy.95), channel_id=1, source_target_pairs={{1,0},{2,1},{3,2},{4,3},{5,4},{6,5},{7,6},{8,7},{9,8},{10,9},{11,1... | collective-permute-start | bytes 3391496 | tf_op jit(solution)/shard_map/ppermute | solution.py:19
  22.6 26.2 %copy-start.2 = (bf16[8,69,2,1024]{3,1,2,0:T(8,128)(2,1)S(1)}, bf16[8,69,2,1024]{3,1,2,0:T(8,128)(2,1)}, u32[]{:S(2)}) copy-start(bf16[8,69,2,1024]{3,1,2,0:T(8,128)(2,1)} %copy.71) | copy-start | bytes 6782980
  48.8 2.6 copy-start.3
  48.8 2.5 copy-start.6
  124.8 103.5 %copy-start.4 = (bf16[3,3,69,256]{3,2,1,0:T(8,128)(2,1)S(1)}, bf16[3,3,69,256]{3,2,1,0:T(8,128)(2,1)}, u32[]{:S(2)}) copy-start(bf16[3,3,69,256]{3,2,1,0:T(8,128)(2,1)} %param.17) | copy-start | bytes 953860
  124.8 103.5 %copy-start.11 = (f32[69]{0:T(128)S(1)}, f32[69]{0:T(128)}, u32[]{:S(2)}) copy-start(f32[69]{0:T(128)} %param.18) | copy-start | bytes 832
  130.8 95.0 %collective-permute-start.2 = (bf16[8,256,1,1024]{3,1,2,0:T(8,128)(2,1)}, bf16[8,256,1,1024]{3,1,2,0:T(8,128)(2,1)}, u32[]{:S(2)}, u32[]{:S(2)}) collective-permute-start(bf16[8,256,1,1024]{3,1,2,0:T(8,128)(2,1)} %get-tuple-element.169), channel_id=1, source_target_pairs={{0,1},{1,2},{2,3},{3,4},{4,5},{5,6},{6,7},{7,8},{8,9},{9,10},{10,1... | collective-permute-start | bytes 12582920 | tf_op jit(solution)/shard_map/ppermute | solution.py:29
  134.3 93.9 %collective-permute-start.3 = (bf16[8,256,1,1024]{3,1,2,0:T(8,128)(2,1)}, bf16[8,256,1,1024]{3,1,2,0:T(8,128)(2,1)}, u32[]{:S(2)}, u32[]{:S(2)}) collective-permute-start(bf16[8,256,1,1024]{3,1,2,0:T(8,128)(2,1)} %get-tuple-element.168), channel_id=1, source_target_pairs={{1,0},{2,1},{3,2},{4,3},{5,4},{6,5},{7,6},{8,7},{9,8},{10,9},{11,1... | collective-permute-start | bytes 12582920 | tf_op jit(solution)/shard_map/ppermute | solution.py:29
  315.7 5.1 copy-start.5
  315.7 53.2 %all-to-all-start = ((bf16[8,69,2,1024]{1,2,0,3:T(2,128)(2,1)}), bf16[8,69,2,1024]{1,2,0,3:T(2,128)(2,1)}, u32[]{:S(2)}, u32[]{:S(2)}) async-start(bf16[8,69,2,1024]{1,2,0,3:T(2,128)(2,1)} %copy.73), calls=%async_computation | async-start | bytes 8388608 | tf_op jit(solution)/shard_map/all_to_all | solution.py:99
  320.7 604.5 %all-gather.3.cloned.1.call-start = ((), (), s32[]{:S(2)}) async-start(), calls=%async_computation.2 | async-start | bytes 8454144 | tf_op jit(solution)/shard_map/all_gather | solution.py:120
  379.4 2.7 copy-start.1
  385.2 159.4 %copy-start.7 = (f32[2,256]{1,0:T(2,128)S(1)}, f32[2,256]{1,0:T(2,128)}, u32[]{:S(2)}) copy-start(f32[2,256]{1,0:T(2,128)} %param.21) | copy-start | bytes 6148
  385.2 159.4 %copy-start.8 = (f32[2,256]{1,0:T(2,128)S(1)}, f32[2,256]{1,0:T(2,128)}, u32[]{:S(2)}) copy-start(f32[2,256]{1,0:T(2,128)} %param.20) | copy-start | bytes 6148
  385.2 177.2 %copy-start.9 = (f32[2,8]{1,0:T(2,128)S(1)}, f32[2,8]{1,0:T(2,128)}, u32[]{:S(2)}) copy-start(f32[2,8]{1,0:T(2,128)} %param.23) | copy-start | bytes 196
  385.2 177.2 %copy-start.10 = (s32[2,8]{1,0:T(2,128)S(1)}, s32[2,8]{1,0:T(2,128)}, u32[]{:S(2)}) copy-start(s32[2,8]{1,0:T(2,128)} %param.22) | copy-start | bytes 196
  546.0 25.5 %all-to-all-start.1 = ((f32[128,2,256]{2,1,0:T(2,128)}), f32[128,2,256]{2,1,0:T(2,128)S(1)}, u32[]{:S(2)}, u32[]{:S(2)}) async-start(f32[128,2,256]{2,1,0:T(2,128)} %stack.2), calls=%async_computation.1 | async-start | bytes 524288 | tf_op jit(solution)/shard_map/all_to_all | solution.py:69
Sparse Core Ops, SparseCore 0:
  545.4 322.1 all-gather.2
